TPU v7x, 32 devices: a whole 2x2x4 slice. The times are simulated.
32 devices in a mesh: lat: 8 (over y, x, core), lon: 4 (over z).
Axes of the slice: x: 2, y: 2, z: 4, core: 2. Of those that a mesh axis runs over, the one named last changes fastest.
Arguments:
- spec_coef: bfloat16 [1280, 2, 64, 1280], P(('lat', 'lon')), may hold values from -0.119628906 to 0.119628906
- legendre: bfloat16 [1280, 128, 1280], P(('lat', 'lon')), may hold values from -0.15625 to 0.15625
- wave_ids: int32 [1280], replicated, may hold values from 0 to 1279, each once
- dep_drow: int32 [128, 5120], P('lat', 'lon'), may hold values from -1 to 1
- dep_dlon: int32 [128, 5120], P('lat', 'lon'), may hold values from -1 to 1
- dep_frac: float32 [2, 128, 5120], P(None, 'lat', 'lon'), may hold values from 0 to 1
Outputs:
- grid: bfloat16 [64, 128, 5120], P(None, 'lat', 'lon')
- departed: bfloat16 [64, 128, 5120], P(None, 'lat', 'lon')
Inputs may be any that keep to these rules, and one draw needn't show every extreme that they name: `wave_ids`: each zonal wavenumber 0 to 1279 stands in exactly one storage row.
All inputs are finite; a program needn't handle non-finite values.
Results may differ from a plain program's by a relative error of at most 0.0059.
Values may be sent and summed in bfloat16 or wider, within the bound.
No kernel may reach another device: no remote copies, remote signals or barrier semaphores. Data moves between devices by JAX's collectives and lax.ppermute only.
A program may use at most 128 MiB of HBM per device.

v0:
```python
import math
import jax
import jax.numpy as jnp
from jax import lax
from jax.sharding import PartitionSpec as P

REACH = 1


def padded_2(cells, sides, width, closed):
    for axis, dim in sides:
        count = lax.axis_size(axis)
        ends = count if closed else count - 1
        head = lax.slice_in_dim(cells, 0, width, axis=dim)
        tail = lax.slice_in_dim(cells, cells.shape[dim] - width, cells.shape[dim], axis=dim)
        cells = jnp.concatenate(
            [
                lax.ppermute(tail, axis, [(i, (i + 1) % count) for i in range(ends)]),
                cells,
                lax.ppermute(head, axis, [((i + 1) % count, i) for i in range(ends)]),
            ],
            axis=dim,
        )
    return cells


def wave_table(wave_order, lon_start, lon_count, cycle_size):
    longitude = lon_start + jnp.arange(lon_count, dtype=jnp.int32)
    phase_index = wave_order[:, None] * longitude[None, :] % cycle_size
    theta = phase_index.astype(jnp.float32) * (2.0 * math.pi / cycle_size)
    factor = jnp.where(wave_order == 0, 1.0, 2.0).astype(jnp.float32)[:, None]
    return jnp.stack([factor * jnp.cos(theta), -factor * jnp.sin(theta)]).astype(jnp.bfloat16)


def shift_weight(offsets, frac, shift):
    zeros = jnp.zeros_like(frac)
    lower = jnp.where(offsets == shift, 1.0 - frac, zeros)
    higher = jnp.where(offsets == shift - 1, frac, zeros)
    return lower + higher


def per_device(spec_coef, legendre, wave_ids, dep_drow, dep_dlon, dep_frac):
    lat_count = lax.axis_size("lat")
    lon_parts = lax.axis_size("lon")
    local_waves = spec_coef.shape[0]
    level_fields = spec_coef.shape[2]
    degree_count = spec_coef.shape[3]
    all_waves = wave_ids.shape[0]
    row_count = dep_drow.shape[0]
    sector_width = dep_drow.shape[1]
    cycle_size = sector_width * lon_parts
    quarter = level_fields // lon_parts
    device = lax.axis_index("lat") * lon_parts + lax.axis_index("lon")
    local_ids = lax.dynamic_slice_in_dim(wave_ids, device * local_waves, local_waves)
    keep = jnp.arange(degree_count, dtype=jnp.int32)[None, :] >= local_ids[:, None]
    kept = jnp.where(keep[:, None, None, :], spec_coef, jnp.zeros((), spec_coef.dtype))
    kept = kept.reshape(local_waves, 2, lon_parts, quarter, degree_count)
    matrices = legendre.reshape(local_waves, lat_count, row_count, degree_count)
    fourier = jnp.einsum(
        "mrbqn,mapn->mabprq", kept, matrices, preferred_element_type=jnp.float32
    ).astype(jnp.bfloat16)
    moved = lax.all_to_all(
        lax.all_to_all(fourier, "lat", split_axis=1, concat_axis=0, tiled=True),
        "lon",
        split_axis=2,
        concat_axis=0,
        tiled=True,
    )
    wave_order = (
        wave_ids.reshape(lat_count, lon_parts, local_waves).transpose(1, 0, 2).reshape(all_waves)
    )
    moved = moved.reshape(all_waves, row_count, 2, quarter)
    table = wave_table(wave_order, lax.axis_index("lon") * sector_width, sector_width, cycle_size)
    grid = jnp.einsum(
        "mprq,rmx->qpx",
        lax.all_gather(moved, "lon", axis=3, tiled=True),
        table,
        preferred_element_type=jnp.float32,
    ).astype(jnp.bfloat16)
    margin = REACH + 1
    tall = padded_2(grid, (("lat", 1),), margin, False)
    padded = padded_2(tall, (("lon", 2),), margin, True)
    frac_row = dep_frac[0]
    frac_col = dep_frac[1]
    col_weights = [shift_weight(dep_dlon, frac_col, shift) for shift in range(-REACH, REACH + 2)]
    total = jnp.zeros((level_fields, row_count, sector_width), jnp.float32)
    for row_shift in range(-REACH, REACH + 2):
        band = padded[:, margin + row_shift : margin + row_shift + row_count, :]
        along = jnp.zeros((level_fields, row_count, sector_width), jnp.float32)
        for place, col_shift in enumerate(range(-REACH, REACH + 2)):
            window = band[:, :, margin + col_shift : margin + col_shift + sector_width].astype(
                jnp.float32
            )
            along = along + col_weights[place][None] * window
        total = total + shift_weight(dep_drow, frac_row, row_shift)[None] * along
    return (grid, total.astype(jnp.bfloat16))


def solution(mesh):
    in_specs = (
        P(("lat", "lon"), None, None, None),
        P(("lat", "lon"), None, None),
        P(),
        P("lat", "lon"),
        P("lat", "lon"),
        P(None, "lat", "lon"),
    )
    out_specs = (P(None, "lat", "lon"), P(None, "lat", "lon"))
    return jax.shard_map(
        per_device, mesh=mesh, in_specs=in_specs, out_specs=out_specs, check_vma=False
    )
```

profile of v0, /device:TPU:5, one launch (start us, length us, event | category | flops | bytes accessed | tf_op | source)
XLA Modules:
  0.0 315.4 jit_solution(18104308854111554694)
XLA Ops:
  7.2 0.0 all-gather.2.cloned.1.call-start
  7.2 0.8 dynamic_slice.3
  8.0 0.1 iota_compare_fusion
  8.1 7.0 %broadcast_select_fusion = bf16[40,2,64,1280]{3,2,1,0:T(8,128)(2,1)S(1)} fusion(bf16[40,2,64,1280]{3,2,1,0:T(8,128)(2,1)} %param.6, pred[40,1280]{1,0:T(8,128)(4,1)S(1)} %iota_compare_fusion), kind=kLoop, calls=%fused_computation | loop fusion | flops 6553600 | bytes 26265600 | tf_op jit(solution)/shard_map/jit(_where)/select_n | solution.py:56
  15.1 19.7 %convert_bitcast_fusion = bf16[40,8,4,16,2,16]{3,5,1,2,4,0:T(8,128)(2,1)} fusion(bf16[40,2,4,16,1280,1]{4,3,5,2,1,0:T(8,128)(2,1)S(1)} %bitcast.93, bf16[40,8,16,1280,1,1]{3,2,1,5,4,0:T(8,128)(2,1)} %bitcast.97), kind=kOutput, calls=%fused_computation.1 | convolution fusion | flops 1678376960 | bytes 27525120 | tf_op jit(solution)/shard_map/mrbqn,mapn->mabprq/dot_general | solution.py:59
  34.9 17.7 %copy.20 = bf16[40,8,4,16,2,16]{0,5,4,3,2,1:T(8,128)(2,1)} copy(bf16[40,8,4,16,2,16]{3,5,1,2,4,0:T(8,128)(2,1)} %convert_bitcast_fusion) | data formatting | bytes 2621440 | tf_op jit(solution)/shard_map/convert_element_type | solution.py:61
  52.6 8.1 %reshape.245 = bf16[8,2,40960]{2,1,0:T(2,128)(2,1)S(1)} reshape(bf16[8,4,16,2,16,40]{5,4,3,2,1,0:T(8,128)(2,1)} %bitcast.92) | data formatting | bytes 2621440
  60.7 20.0 %all_to_all.33 = bf16[8,2,40960]{2,1,0:T(2,128)(2,1)S(1)} all-to-all(bf16[8,2,40960]{2,1,0:T(2,128)(2,1)S(1)} %reshape.245), channel_id=1, replica_groups=mesh['lat'=8,'lon'=4] {'lat'}, dimensions={0} | all-to-all | bytes 2621440 | tf_op jit(solution)/shard_map/all_to_all | solution.py:63
  80.7 7.2 %reshape.246 = bf16[8,4,16,2,16,40]{5,4,3,2,1,0:T(8,128)(2,1)} reshape(bf16[8,2,40960]{2,1,0:T(2,128)(2,1)S(1)} %all_to_all.33) | data formatting | bytes 2621440
  87.9 3.0 bitcast_bitcast_fusion
  90.9 6.8 %copy.21 = bf16[8,40,1,4,16,2,16]{1,0,6,5,4,3,2:T(8,128)(2,1)} copy(bf16[8,40,1,4,16,2,16]{1,6,5,4,3,0,2:T(8,128)(2,1)S(1)} %bitcast_bitcast_fusion) | data formatting | bytes 2621440 | tf_op jit(solution)/shard_map/all_to_all | solution.py:63
  97.7 5.5 %all_to_all.27 = bf16[320,1,4,16,2,16]{0,5,4,3,2,1:T(8,128)(2,1)S(1)} reshape(bf16[8,40,1,4,16,2,16]{1,0,6,5,4,3,2:T(8,128)(2,1)} %copy.21) | data formatting | bytes 2621440 | tf_op jit(solution)/shard_map/all_to_all | solution.py:63
  103.2 0.0 copy-start.3
  103.2 40.5 %all_to_all.34 = bf16[320,1,4,16,2,16]{0,5,4,3,1,2:T(8,128)(2,1)S(1)} all-to-all(bf16[320,1,4,16,2,16]{0,5,4,3,1,2:T(8,128)(2,1)S(1)} %bitcast.95), channel_id=1, replica_groups=mesh['lat'=8,'lon'=4] {'lon'}, dimensions={2} | all-to-all | bytes 2621440 | tf_op jit(solution)/shard_map/all_to_all | solution.py:62
  143.8 1.2 copy.23
  145.0 2.1 reshape.240
  147.0 0.0 all-gather.2.cloned.1.call-update
  147.1 0.0 copy-done.3
  147.1 0.1 reshape.236
  147.2 0.1 reshape.237
  147.3 29.5 %multiply_convert_fusion.1 = (bf16[1,1280,1280]{2,1,0:T(8,128)(2,1)S(1)}, bf16[1,1280,1280]{2,1,0:T(8,128)(2,1)}) fusion(s32[1280]{0:T(1024)S(1)} %iota_add_fusion, s32[1280]{0:T(1024)S(1)} %reshape.237, f32[1280]{0:T(1024)S(1)} %get-tuple-element.30, f32[1280]{0:T(1024)S(1)} %get-tuple-element.31), kind=kLoop, calls=%fused_computation.10 | loop fusion | flops 21299200 | bytes 6574080 | tf_op jit(solution)/shard_map/convert
  176.8 68.7 %all-gather.2.cloned.1.call-done = bf16[1280,16,2,64]{0,3,2,1:T(8,128)(2,1)} async-done(((bf16[1280,16,2,16]{0,3,2,1:T(8,128)(2,1)}), bf16[1280,16,2,64]{0,3,2,1:T(8,128)(2,1)}) %all-gather.2.cloned.1.call-update) | async-done | bytes 5242896 | tf_op jit(solution)/shard_map/all_gather | solution.py:76
  245.6 9.9 %fusion.8 = bf16[64,16,1280]{2,0,1:T(8,128)(2,1)S(1)} fusion(bf16[1280,16,2,64]{0,3,2,1:T(8,128)(2,1)} %all-gather.2.cloned.1.call-done, bf16[1,1280,1280]{2,1,0:T(8,128)(2,1)} %get-tuple-element.29, bf16[1,1280,1280]{2,1,0:T(8,128)(2,1)S(1)} %get-tuple-element.28), kind=kOutput, calls=%fused_computation.19 | convolution fusion | flops 6725304320 | bytes 14417920 | tf_op jit(solution)/shard_map/mprq,rmx->qpx/dot_general | solution.py:74
  255.5 0.0 copy-start
  255.5 0.0 copy-start.1
  255.5 0.0 copy-start.2
  255.6 3.6 %collective-permute-start = (bf16[64,2,1280]{2,0,1:T(8,128)(2,1)S(1)}, bf16[64,2,1280]{2,0,1:T(8,128)(2,1)S(1)}, u32[]{:S(2)}, u32[]{:S(2)}) collective-permute-start(bf16[64,2,1280]{2,0,1:T(8,128)(2,1)S(1)} %get-tuple-element.14), channel_id=1, source_target_pairs={{0,4},{4,8},{8,12},{12,16},{16,20},{20,24},{24,28},{1,5},{5,9},{9,... | collective-permute-start | bytes 983048 | tf_op jit(solution)/shard_map/ppermute | solution.py:18
  259.2 1.9 collective-permute-start.1
  261.1 2.1 collective-permute-done
  263.2 4.4 %collective-permute-done.1 = bf16[64,2,1280]{2,0,1:T(8,128)(2,1)S(1)} collective-permute-done((bf16[64,2,1280]{2,0,1:T(8,128)(2,1)S(1)}, bf16[64,2,1280]{2,0,1:T(8,128)(2,1)S(1)}, u32[]{:S(2)}, u32[]{:S(2)}) %collective-permute-start.1) | collective-permute-done | bytes 327712 | tf_op jit(solution)/shard_map/ppermute | solution.py:20
  267.6 0.2 pad_maximum_fusion.5
  267.8 0.1 collective-permute-start.2
  267.8 3.3 %collective-permute-start.3 = (bf16[64,20,2]{2,0,1:T(8,128)(2,1)S(1)}, bf16[64,20,2]{2,0,1:T(8,128)(2,1)S(1)}, u32[]{:S(2)}, u32[]{:S(2)}) collective-permute-start(bf16[64,20,2]{2,0,1:T(8,128)(2,1)S(1)} %get-tuple-element.13), channel_id=1, source_target_pairs={{1,0},{2,1},{3,2},{0,3},{5,4},{6,5},{7,6},{4,7},{9,8},{10,9},{11,1... | collective-permute-start | bytes 15368 | tf_op jit(solution)/shard_map/ppermute | solution.py:20
  271.1 0.0 copy-done
  271.1 0.0 copy-done.1
  271.1 0.0 copy-done.2
  271.1 0.1 fusion.14
  271.2 2.9 copy.24
  274.1 5.1 %collective-permute-done.2 = bf16[64,20,2]{2,0,1:T(8,128)(2,1)S(1)} collective-permute-done((bf16[64,20,2]{2,0,1:T(8,128)(2,1)S(1)}, bf16[64,20,2]{2,0,1:T(8,128)(2,1)S(1)}, u32[]{:S(2)}, u32[]{:S(2)}) %collective-permute-start.2) | collective-permute-done | bytes 5152 | tf_op jit(solution)/shard_map/ppermute | solution.py:18
  279.3 5.5 %collective-permute-done.3 = bf16[64,20,2]{2,0,1:T(8,128)(2,1)S(1)} collective-permute-done((bf16[64,20,2]{2,0,1:T(8,128)(2,1)S(1)}, bf16[64,20,2]{2,0,1:T(8,128)(2,1)S(1)}, u32[]{:S(2)}, u32[]{:S(2)}) %collective-permute-start.3) | collective-permute-done | bytes 5152 | tf_op jit(solution)/shard_map/ppermute | solution.py:20
  284.8 2.7 maximum_maximum_fusion
  287.5 18.1 %add_convert_fusion = bf16[64,16,1280]{2,0,1:T(8,128)(2,1)S(1)} fusion(bf16[64,16,1280]{2,0,1:T(8,128)(2,1)S(1)} %fusion.8, bf16[64,2,1280]{2,0,1:T(8,128)(2,1)S(1)} %collective-permute-done.1, bf16[64,20,1282]{2,0,1:T(8,128)(2,1)S(1)} %get-tuple-element.11, bf16[64,20,1282]{2,0,1:T(8,128)(2,1)S(1)} %get-tuple-element.10, ...), kind=kLoop, calls=%fused_computation.16 | loop fusion | flops 72089600 | bytes 38010880 | tf_op jit(solution)/shard_map/convert_element_type | solution.py:96
  305.6 2.9 copy.25
  (4 shorter events, 0.1 us)
Async XLA Ops:
  7.2 238.4 %all-gather.2.cloned.1.call-start = ((), (), s32[]{:S(2)}) async-start(), calls=%async_computation.2 | async-start | bytes 6553600 | tf_op jit(solution)/shard_map/all_gather | solution.py:76
  103.2 43.8 %copy-start.3 = (s32[1280]{0:T(1024)S(1)}, s32[1280]{0:T(1024)}, u32[]{:S(2)}) copy-start(s32[1280]{0:T(1024)} %param.8) | copy-start | bytes 15364
  255.5 15.6 %copy-start = (f32[2,16,1280]{2,1,0:T(8,128)S(1)}, f32[2,16,1280]{2,1,0:T(8,128)}, u32[]{:S(2)}) copy-start(f32[2,16,1280]{2,1,0:T(8,128)} %param.11) | copy-start | bytes 491524
  255.5 15.6 %copy-start.1 = (s32[16,1280]{1,0:T(8,128)S(1)}, s32[16,1280]{1,0:T(8,128)}, u32[]{:S(2)}) copy-start(s32[16,1280]{1,0:T(8,128)} %param.9) | copy-start | bytes 245764
  255.5 15.6 %copy-start.2 = (s32[16,1280]{1,0:T(8,128)S(1)}, s32[16,1280]{1,0:T(8,128)}, u32[]{:S(2)}) copy-start(s32[16,1280]{1,0:T(8,128)} %param.10) | copy-start | bytes 245764
  255.6 7.6 %collective-permute-start = (bf16[64,2,1280]{2,0,1:T(8,128)(2,1)S(1)}, bf16[64,2,1280]{2,0,1:T(8,128)(2,1)S(1)}, u32[]{:S(2)}, u32[]{:S(2)}) collective-permute-start(bf16[64,2,1280]{2,0,1:T(8,128)(2,1)S(1)} %get-tuple-element.14), channel_id=1, source_target_pairs={{0,4},{4,8},{8,12},{12,16},{16,20},{20,24},{24,28},{1,5},{5,9},{9,... | collective-permute-start | bytes 983048 | tf_op jit(solution)/shard_map/ppermute | solution.py:18
  259.2 8.4 %collective-permute-start.1 = (bf16[64,2,1280]{2,0,1:T(8,128)(2,1)S(1)}, bf16[64,2,1280]{2,0,1:T(8,128)(2,1)S(1)}, u32[]{:S(2)}, u32[]{:S(2)}) collective-permute-start(bf16[64,2,1280]{2,0,1:T(8,128)(2,1)S(1)} %get-tuple-element.15), channel_id=1, source_target_pairs={{4,0},{8,4},{12,8},{16,12},{20,16},{24,20},{28,24},{5,1},{9,5},{13... | collective-permute-start | bytes 983048 | tf_op jit(solution)/shard_map/ppermute | solution.py:20
  267.8 11.5 %collective-permute-start.2 = (bf16[64,20,2]{2,0,1:T(8,128)(2,1)S(1)}, bf16[64,20,2]{2,0,1:T(8,128)(2,1)S(1)}, u32[]{:S(2)}, u32[]{:S(2)}) collective-permute-start(bf16[64,20,2]{2,0,1:T(8,128)(2,1)S(1)} %get-tuple-element.12), channel_id=1, source_target_pairs={{0,1},{1,2},{2,3},{3,0},{4,5},{5,6},{6,7},{7,4},{8,9},{9,10},{10,1... | collective-permute-start | bytes 15368 | tf_op jit(solution)/shard_map/ppermute | solution.py:18
  267.8 16.9 %collective-permute-start.3 = (bf16[64,20,2]{2,0,1:T(8,128)(2,1)S(1)}, bf16[64,20,2]{2,0,1:T(8,128)(2,1)S(1)}, u32[]{:S(2)}, u32[]{:S(2)}) collective-permute-start(bf16[64,20,2]{2,0,1:T(8,128)(2,1)S(1)} %get-tuple-element.13), channel_id=1, source_target_pairs={{1,0},{2,1},{3,2},{0,3},{5,4},{6,5},{7,6},{4,7},{9,8},{10,9},{11,1... | collective-permute-start | bytes 15368 | tf_op jit(solution)/shard_map/ppermute | solution.py:20
Sparse Core Ops, SparseCore 0:
  147.2 98.3 all-gather.1
where the time goes:
time: 316 us; the launch traced here: 315 us
  waiting for transfers between devices  85.9 us (27%)
  blocking collectives  60.6 us (19%)
  local copies, waits for them, and re-layouts  58.5 us (19%)
  other arithmetic  57.8 us (18%)
  matrix products  29.6 us (9%)
  between operations  14.2 us (4%)
  starting transfers between devices  8.87 us (3%)
    all_gather x1, waiting for transfers between devices, per_device(): lax.all_gather(moved, 'lon', axis=3, tiled=True)  68.7 us
    all_to_all x1, blocking collectives, per_device(): lax.all_to_all(lax.all_to_all(fourier, 'lat', split_axis=1, concat_axis=0...  40.5 us
    another operation x1, other arithmetic  29.5 us
    unnamed x12, local copies, waits for them, and re-layouts  21.2 us
    all_to_all x1, blocking collectives, per_device(): lax.all_to_all(fourier, 'lat', split_axis=1, concat_axis=0, tiled=True)  20 us
    dot_general x1, matrix products, per_device(): jnp.einsum('mrbqn,mapn->mabprq', kept, matrices, preferred_element_type=j...  19.7 us
    convert_element_type x1, other arithmetic, per_device(): return (grid, total.astype(jnp.bfloat16))  18.1 us
    convert_element_type x1, local copies, waits for them, and re-layouts, per_device(): fourier = jnp.einsum('mrbqn,mapn->mabprq', kept, matrices, preferred_elem...  17.7 us
  transfers between devices with their start and end apart: 5, of which 5 were waited for; matrix products, arithmetic and copies ran while one was open for 10% of the time, Pallas kernels for 0%

commit v1 on v0

--- a/solution.py
+++ b/solution.py
@@ -60,7 +60,12 @@
         "mrbqn,mapn->mabprq", kept, matrices, preferred_element_type=jnp.float32
     ).astype(jnp.bfloat16)
     moved = lax.all_to_all(
-        lax.all_to_all(fourier, "lat", split_axis=1, concat_axis=0, tiled=True),
+        jnp.concatenate(
+            lax.all_to_all(
+                jnp.stack(jnp.split(fourier, lax.axis_size("lat"), axis=1)), "lat", 0, 0
+            ),
+            axis=0,
+        ),
         "lon",
         split_axis=2,
         concat_axis=0,

time: 316 us -> 336 us (1.063)
  local copies, waits for them, and re-layouts: 58.5 us -> 80.1 us
    another operation x0 -> x10, local copies, waits for them, and re-layouts: none -> 30.1 us  [per_device(): jnp.stack(jnp.split(fourier, lax.axis_size('lat'), axis=1))]
    convert_element_type x1 -> x0, local copies, waits for them, and re-layouts: 17.7 us -> none  [per_device(): fourier = jnp.einsum('mrbqn,mapn->mabprq', kept, matrices, preferred_elem...]
    unnamed x12 -> x23, local copies, waits for them, and re-layouts: 21.2 us -> 31.2 us
    all_to_all x4 -> x2, local copies, waits for them, and re-layouts: 16.5 us -> 10.2 us  [the longest x1 9.03 us: per_device(): lax.all_to_all(jnp.stack(jnp.split(fourier, lax.axis_size('lat'), axis=1)...]
    reshape x0 -> x1, local copies, waits for them, and re-layouts: none -> 5.5 us  [per_device(): jnp.concatenate(lax.all_to_all(jnp.stack(jnp.split(fourier, lax.axis_size...]
where the time goes in v1:
time: 336 us; the launch traced here: 335 us
  waiting for transfers between devices  85.6 us (25%)
  local copies, waits for them, and re-layouts  80.1 us (24%)
  blocking collectives  60.6 us (18%)
  other arithmetic  57.8 us (17%)
  matrix products  28.2 us (8%)
  between operations  14.3 us (4%)
  starting transfers between devices  8.87 us (3%)
    all_gather x1, waiting for transfers between devices, per_device(): lax.all_gather(moved, 'lon', axis=3, tiled=True)  68.7 us
    all_to_all x1, blocking collectives, per_device(): lax.all_to_all(jnp.concatenate(lax.all_to_all(jnp.stack(jnp.split(fourier...  40.5 us
    unnamed x23, local copies, waits for them, and re-layouts  31.2 us
    another operation x10, local copies, waits for them, and re-layouts, per_device(): jnp.stack(jnp.split(fourier, lax.axis_size('lat'), axis=1))  30.1 us
    another operation x1, other arithmetic  29.6 us
    all_to_all x1, blocking collectives, per_device(): lax.all_to_all(jnp.stack(jnp.split(fourier, lax.axis_size('lat'), axis=1)...  20.1 us
    dot_general x1, matrix products, per_device(): jnp.einsum('mrbqn,mapn->mabprq', kept, matrices, preferred_element_type=j...  18.4 us
    convert_element_type x1, other arithmetic, per_device(): return (grid, total.astype(jnp.bfloat16))  18.1 us
  transfers between devices with their start and end apart: 5, of which 5 were waited for; matrix products, arithmetic and copies ran while one was open for 10% of the time, Pallas kernels for 0%

profile of v1, /device:TPU:5, one launch (start us, length us, event | category | flops | bytes accessed | tf_op | source)
XLA Modules:
  0.0 335.4 jit_solution(1477870000359007491)
XLA Ops:
  7.2 0.0 all-gather.2.cloned.1.call-start
  7.2 0.8 dynamic_slice.3
  8.0 0.1 iota_compare_fusion
  8.1 7.0 %broadcast_select_fusion = bf16[40,2,64,1280]{3,2,1,0:T(8,128)(2,1)S(1)} fusion(bf16[40,2,64,1280]{3,2,1,0:T(8,128)(2,1)} %param.6, pred[40,1280]{1,0:T(8,128)(4,1)S(1)} %iota_compare_fusion), kind=kLoop, calls=%fused_computation | loop fusion | flops 6553600 | bytes 26265600 | tf_op jit(solution)/shard_map/jit(_where)/select_n | solution.py:56
  15.1 18.4 %convert_bitcast_fusion = bf16[40,8,4,16,2,16]{3,5,1,2,4,0:T(8,128)(2,1)S(1)} fusion(bf16[40,2,4,16,1280,1]{4,3,5,2,1,0:T(8,128)(2,1)S(1)} %bitcast.104, bf16[40,8,16,1280,1,1]{3,2,1,5,4,0:T(8,128)(2,1)} %bitcast.109), kind=kOutput, calls=%fused_computation.1 | convolution fusion | flops 1678376960 | bytes 27525120 | tf_op jit(solution)/shard_map/mrbqn,mapn->mabprq/dot_general | solution.py:59
  33.5 4.3 %slice_bitcast_fusion = (bf16[1,40,1,4,16,2,16]{4,6,3,5,1,2,0:T(8,128)(2,1)S(1)}, bf16[1,40,1,4,16,2,16]{4,6,3,5,1,2,0:T(8,128)(2,1)}, bf16[1,40,1,4,16,2,16]{4,...) fusion(bf16[40,8,4,16,2,16]{3,5,1,2,4,0:T(8,128)(2,1)S(1)} %con, ...), kind=kLoop, calls=%fused_computation.25 | loop fusion | bytes 2621440 | tf_op jit(solution)/shard_map/stack | solution.py:65
  37.8 3.0 copy.52
  40.8 0.0 copy-start
  40.8 0.8 constant_dynamic-update-slice_fusion.7
  41.7 3.7 %copy.53 = bf16[1,40,1,4,16,2,16]{1,6,5,4,3,2,0:T(8,128)(2,1)} copy(bf16[1,40,1,4,16,2,16]{4,6,3,5,1,2,0:T(8,128)(2,1)} %get-tuple-element.18) | data formatting | bytes 327680 | tf_op jit(solution)/shard_map/stack | solution.py:65
  45.3 3.7 %copy.54 = bf16[1,40,1,4,16,2,16]{1,6,5,4,3,2,0:T(8,128)(2,1)} copy(bf16[1,40,1,4,16,2,16]{4,6,3,5,1,2,0:T(8,128)(2,1)} %get-tuple-element.17) | data formatting | bytes 327680 | tf_op jit(solution)/shard_map/stack | solution.py:65
  49.0 3.6 %copy.55 = bf16[1,40,1,4,16,2,16]{1,6,5,4,3,2,0:T(8,128)(2,1)} copy(bf16[1,40,1,4,16,2,16]{4,6,3,5,1,2,0:T(8,128)(2,1)} %get-tuple-element.16) | data formatting | bytes 327680 | tf_op jit(solution)/shard_map/stack | solution.py:65
  52.6 3.6 %copy.56 = bf16[1,40,1,4,16,2,16]{1,6,5,4,3,2,0:T(8,128)(2,1)} copy(bf16[1,40,1,4,16,2,16]{4,6,3,5,1,2,0:T(8,128)(2,1)} %get-tuple-element.15) | data formatting | bytes 327680 | tf_op jit(solution)/shard_map/stack | solution.py:65
  56.2 3.7 %copy.57 = bf16[1,40,1,4,16,2,16]{1,6,5,4,3,2,0:T(8,128)(2,1)} copy(bf16[1,40,1,4,16,2,16]{4,6,3,5,1,2,0:T(8,128)(2,1)} %get-tuple-element.14) | data formatting | bytes 327680 | tf_op jit(solution)/shard_map/stack | solution.py:65
  59.9 0.0 copy-done
  59.9 1.8 copy.58
  61.8 0.0 copy-start.1
  61.8 1.9 copy.59
  63.6 1.9 constant_dynamic-update-slice_fusion.6
  65.5 1.9 constant_dynamic-update-slice_fusion.5
  67.4 1.9 constant_dynamic-update-slice_fusion.4
  69.3 1.9 constant_dynamic-update-slice_fusion.3
  71.2 0.0 copy-done.1
  71.2 0.8 constant_dynamic-update-slice_fusion.2
  72.0 0.8 constant_dynamic-update-slice_fusion.1
  72.8 0.8 constant_dynamic-update-slice_fusion
  73.7 8.1 %reshape.249 = bf16[8,2,40960]{2,1,0:T(2,128)(2,1)S(1)} reshape(bf16[8,1,4,16,2,16,40]{6,5,4,3,2,1,0:T(8,128)(2,1)} %bitcast.107) | data formatting | bytes 2621440
  81.8 20.1 %all_to_all.20 = bf16[8,2,40960]{2,1,0:T(2,128)(2,1)S(1)} all-to-all(bf16[8,2,40960]{2,1,0:T(2,128)(2,1)S(1)} %reshape.249), channel_id=1, replica_groups=mesh['lat'=8,'lon'=4] {'lat'}, dimensions={0} | all-to-all | bytes 2621440 | tf_op jit(solution)/shard_map/all_to_all | solution.py:64
  101.9 7.2 %reshape.250 = bf16[8,1,4,16,2,16,40]{6,5,4,3,2,1,0:T(8,128)(2,1)} reshape(bf16[8,2,40960]{2,1,0:T(2,128)(2,1)S(1)} %all_to_all.20) | data formatting | bytes 2621440
  109.0 9.0 %copy.60 = bf16[8,40,1,4,16,2,16]{1,0,6,5,4,3,2:T(8,128)(2,1)} copy(bf16[8,40,1,4,16,2,16]{1,6,5,4,3,2,0:T(8,128)(2,1)} %bitcast.103) | data formatting | bytes 2621440 | tf_op jit(solution)/shard_map/all_to_all | solution.py:64
  118.1 5.5 %reshape.243 = bf16[320,1,4,16,2,16]{0,5,4,3,2,1:T(8,128)(2,1)S(1)} reshape(bf16[8,40,1,4,16,2,16]{1,0,6,5,4,3,2:T(8,128)(2,1)} %copy.60) | data formatting | bytes 2621440 | tf_op jit(solution)/shard_map/reshape | solution.py:63
  123.6 0.0 copy-start.5
  123.6 40.5 %all_to_all.21 = bf16[320,1,4,16,2,16]{0,5,4,3,1,2:T(8,128)(2,1)S(1)} all-to-all(bf16[320,1,4,16,2,16]{0,5,4,3,1,2:T(8,128)(2,1)S(1)} %bitcast.106), channel_id=1, replica_groups=mesh['lat'=8,'lon'=4] {'lon'}, dimensions={2} | all-to-all | bytes 2621440 | tf_op jit(solution)/shard_map/all_to_all | solution.py:62
  164.1 1.2 copy.62
  165.3 2.1 reshape.244
  167.4 0.0 all-gather.2.cloned.1.call-update
  167.4 0.0 copy-done.5
  167.4 0.1 reshape.239
  167.5 0.1 reshape.240
  167.6 29.6 %multiply_convert_fusion.1 = (bf16[1,1280,1280]{2,1,0:T(8,128)(2,1)S(1)}, bf16[1,1280,1280]{2,1,0:T(8,128)(2,1)}) fusion(s32[1280]{0:T(1024)S(1)} %iota_add_fusion, s32[1280]{0:T(1024)S(1)} %reshape.240, f32[1280]{0:T(1024)S(1)} %get-tuple-element.40, f32[1280]{0:T(1024)S(1)} %get-tuple-element.41), kind=kLoop, calls=%fused_computation.10 | loop fusion | flops 21299200 | bytes 6574080 | tf_op jit(solution)/shard_map/convert
  197.2 68.7 %all-gather.2.cloned.1.call-done = bf16[1280,16,2,64]{0,3,2,1:T(8,128)(2,1)} async-done(((bf16[1280,16,2,16]{0,3,2,1:T(8,128)(2,1)}), bf16[1280,16,2,64]{0,3,2,1:T(8,128)(2,1)}) %all-gather.2.cloned.1.call-update) | async-done | bytes 5242896 | tf_op jit(solution)/shard_map/all_gather | solution.py:81
  265.9 9.9 %fusion.8 = bf16[64,16,1280]{2,0,1:T(8,128)(2,1)S(1)} fusion(bf16[1280,16,2,64]{0,3,2,1:T(8,128)(2,1)} %all-gather.2.cloned.1.call-done, bf16[1,1280,1280]{2,1,0:T(8,128)(2,1)} %get-tuple-element.39, bf16[1,1280,1280]{2,1,0:T(8,128)(2,1)S(1)} %get-tuple-element.38), kind=kOutput, calls=%fused_computation.19 | convolution fusion | flops 6725304320 | bytes 14417920 | tf_op jit(solution)/shard_map/mprq,rmx->qpx/dot_general | solution.py:79
  275.8 0.0 copy-start.2
  275.8 0.0 copy-start.3
  275.8 0.0 copy-start.4
  275.9 3.6 %collective-permute-start = (bf16[64,2,1280]{2,0,1:T(8,128)(2,1)S(1)}, bf16[64,2,1280]{2,0,1:T(8,128)(2,1)S(1)}, u32[]{:S(2)}, u32[]{:S(2)}) collective-permute-start(bf16[64,2,1280]{2,0,1:T(8,128)(2,1)S(1)} %get-tuple-element.24), channel_id=1, source_target_pairs={{0,4},{4,8},{8,12},{12,16},{16,20},{20,24},{24,28},{1,5},{5,9},{9,... | collective-permute-start | bytes 983048 | tf_op jit(solution)/shard_map/ppermute | solution.py:18
  279.5 1.9 collective-permute-start.1
  281.4 2.1 collective-permute-done
  283.5 4.4 %collective-permute-done.1 = bf16[64,2,1280]{2,0,1:T(8,128)(2,1)S(1)} collective-permute-done((bf16[64,2,1280]{2,0,1:T(8,128)(2,1)S(1)}, bf16[64,2,1280]{2,0,1:T(8,128)(2,1)S(1)}, u32[]{:S(2)}, u32[]{:S(2)}) %collective-permute-start.1) | collective-permute-done | bytes 327712 | tf_op jit(solution)/shard_map/ppermute | solution.py:20
  287.9 0.2 pad_maximum_fusion.5
  288.1 0.1 collective-permute-start.2
  288.2 3.3 collective-permute-start.3
  291.4 0.0 copy-done.2
  291.4 0.0 copy-done.3
  291.4 0.0 copy-done.4
  291.4 0.1 fusion.14
  291.5 2.9 copy.63
  294.4 5.1 %collective-permute-done.2 = bf16[64,20,2]{2,0,1:T(8,128)(2,1)S(1)} collective-permute-done((bf16[64,20,2]{2,0,1:T(8,128)(2,1)S(1)}, bf16[64,20,2]{2,0,1:T(8,128)(2,1)S(1)}, u32[]{:S(2)}, u32[]{:S(2)}) %collective-permute-start.2) | collective-permute-done | bytes 5152 | tf_op jit(solution)/shard_map/ppermute | solution.py:18
  299.6 5.2 %collective-permute-done.3 = bf16[64,20,2]{2,0,1:T(8,128)(2,1)S(1)} collective-permute-done((bf16[64,20,2]{2,0,1:T(8,128)(2,1)S(1)}, bf16[64,20,2]{2,0,1:T(8,128)(2,1)S(1)}, u32[]{:S(2)}, u32[]{:S(2)}) %collective-permute-start.3) | collective-permute-done | bytes 5152 | tf_op jit(solution)/shard_map/ppermute | solution.py:20
  304.8 2.7 maximum_maximum_fusion
  307.5 18.1 %add_convert_fusion = bf16[64,16,1280]{2,0,1:T(8,128)(2,1)S(1)} fusion(bf16[64,16,1280]{2,0,1:T(8,128)(2,1)S(1)} %fusion.8, bf16[64,2,1280]{2,0,1:T(8,128)(2,1)S(1)} %collective-permute-done.1, bf16[64,20,1282]{2,0,1:T(8,128)(2,1)S(1)} %get-tuple-element.21, bf16[64,20,1282]{2,0,1:T(8,128)(2,1)S(1)} %get-tuple-element.20, ...), kind=kLoop, calls=%fused_computation.16 | loop fusion | flops 72089600 | bytes 38010880 | tf_op jit(solution)/shard_map/convert_element_type | solution.py:101
  325.7 2.9 copy.64
  (4 shorter events, 0.1 us)
Async XLA Ops:
  7.2 258.7 %all-gather.2.cloned.1.call-start = ((), (), s32[]{:S(2)}) async-start(), calls=%async_computation.2 | async-start | bytes 6553600 | tf_op jit(solution)/shard_map/all_gather | solution.py:81
  40.8 19.1 %copy-start = (bf16[1,40,1,4,16,2,16]{4,6,3,5,1,2,0:T(8,128)(2,1)S(1)}, bf16[1,40,1,4,16,2,16]{4,6,3,5,1,2,0:T(8,128)(2,1)}, u32[]{:S(2)}) copy-start(bf16[1,40,1,4,16,2,16]{4,6,3,5,1,2,0:T(8,128)(2,1)} %get-tuple-element.13) | copy-start | bytes 491524
  61.8 9.4 %copy-start.1 = (bf16[1,40,1,4,16,2,16]{1,6,5,4,3,2,0:T(8,128)(2,1)S(1)}, bf16[1,40,1,4,16,2,16]{1,6,5,4,3,2,0:T(8,128)(2,1)}, u32[]{:S(2)}) copy-start(bf16[1,40,1,4,16,2,16]{1,6,5,4,3,2,0:T(8,128)(2,1)} %copy.57) | copy-start | bytes 491524
  123.6 43.8 %copy-start.5 = (s32[1280]{0:T(1024)S(1)}, s32[1280]{0:T(1024)}, u32[]{:S(2)}) copy-start(s32[1280]{0:T(1024)} %param.8) | copy-start | bytes 15364
  275.8 15.6 %copy-start.2 = (f32[2,16,1280]{2,1,0:T(8,128)S(1)}, f32[2,16,1280]{2,1,0:T(8,128)}, u32[]{:S(2)}) copy-start(f32[2,16,1280]{2,1,0:T(8,128)} %param.11) | copy-start | bytes 491524
  275.8 15.6 %copy-start.3 = (s32[16,1280]{1,0:T(8,128)S(1)}, s32[16,1280]{1,0:T(8,128)}, u32[]{:S(2)}) copy-start(s32[16,1280]{1,0:T(8,128)} %param.9) | copy-start | bytes 245764
  275.8 15.6 %copy-start.4 = (s32[16,1280]{1,0:T(8,128)S(1)}, s32[16,1280]{1,0:T(8,128)}, u32[]{:S(2)}) copy-start(s32[16,1280]{1,0:T(8,128)} %param.10) | copy-start | bytes 245764
  275.9 7.6 %collective-permute-start = (bf16[64,2,1280]{2,0,1:T(8,128)(2,1)S(1)}, bf16[64,2,1280]{2,0,1:T(8,128)(2,1)S(1)}, u32[]{:S(2)}, u32[]{:S(2)}) collective-permute-start(bf16[64,2,1280]{2,0,1:T(8,128)(2,1)S(1)} %get-tuple-element.24), channel_id=1, source_target_pairs={{0,4},{4,8},{8,12},{12,16},{16,20},{20,24},{24,28},{1,5},{5,9},{9,... | collective-permute-start | bytes 983048 | tf_op jit(solution)/shard_map/ppermute | solution.py:18
  279.5 8.4 %collective-permute-start.1 = (bf16[64,2,1280]{2,0,1:T(8,128)(2,1)S(1)}, bf16[64,2,1280]{2,0,1:T(8,128)(2,1)S(1)}, u32[]{:S(2)}, u32[]{:S(2)}) collective-permute-start(bf16[64,2,1280]{2,0,1:T(8,128)(2,1)S(1)} %get-tuple-element.25), channel_id=1, source_target_pairs={{4,0},{8,4},{12,8},{16,12},{20,16},{24,20},{28,24},{5,1},{9,5},{13... | collective-permute-start | bytes 983048 | tf_op jit(solution)/shard_map/ppermute | solution.py:20
  288.1 11.5 %collective-permute-start.2 = (bf16[64,20,2]{2,0,1:T(8,128)(2,1)S(1)}, bf16[64,20,2]{2,0,1:T(8,128)(2,1)S(1)}, u32[]{:S(2)}, u32[]{:S(2)}) collective-permute-start(bf16[64,20,2]{2,0,1:T(8,128)(2,1)S(1)} %get-tuple-element.22), channel_id=1, source_target_pairs={{0,1},{1,2},{2,3},{3,0},{4,5},{5,6},{6,7},{7,4},{8,9},{9,10},{10,1... | collective-permute-start | bytes 15368 | tf_op jit(solution)/shard_map/ppermute | solution.py:18
  288.2 16.7 %collective-permute-start.3 = (bf16[64,20,2]{2,0,1:T(8,128)(2,1)S(1)}, bf16[64,20,2]{2,0,1:T(8,128)(2,1)S(1)}, u32[]{:S(2)}, u32[]{:S(2)}) collective-permute-start(bf16[64,20,2]{2,0,1:T(8,128)(2,1)S(1)} %get-tuple-element.23), channel_id=1, source_target_pairs={{1,0},{2,1},{3,2},{0,3},{5,4},{6,5},{7,6},{4,7},{9,8},{10,9},{11,1... | collective-permute-start | bytes 15368 | tf_op jit(solution)/shard_map/ppermute | solution.py:20
Sparse Core Ops, SparseCore 0:
  167.5 98.3 all-gather.1
